TPU v7x, 256 devices: a whole 4x4x8 slice. The times are simulated.
256 devices in a mesh: wide: 64 (over y, z, core), col: 4 (over x).
Axes of the slice: x: 4, y: 4, z: 8, core: 2. Of those that a mesh axis runs over, the one named last changes fastest.
Arguments:
- assembled: float32 [9216, 1024], P(('wide', 'col')), as said below
- row_map: int32 [9216], P(('wide', 'col')), may hold values from 0 to 9215, as said below
- fill_pattern: int32 [2, 32], replicated, may hold values from 0 to 1
- trailing_block: float32 [64, 4, 32, 8192], P(None, 'col', None, 'wide'), may hold values from -6 to 6
Outputs:
- schur: float32 [64, 4, 32, 8192], P(None, 'col', None, 'wide')
- panel_rows: float32 [8192, 1024], P(('wide', 'col'))
- diag_factor: float32 [1024, 1024], P(('wide', 'col'))
Inputs may be any that keep to these rules, and one draw needn't show every extreme that they name: row_map is a permutation of the window rows. Each device, with col index c, holds exactly 32 trailing rows 1024 + t whose owner device index t // 32 has col index c, and exactly 4 rows d below 1024 with d // 256 equal to c. At most 2 of one device's trailing rows have the same owner, and every device holds exactly 2 trailing rows of some owner. `assembled`: D is symmetric positive definite.
All inputs are finite; a program needn't handle non-finite values.
Results may differ from a plain program's by a relative error of at most 0.00008.
Values sent between devices are 32-bit elements; how exact they have to be, the bound alone decides.
No kernel may reach another device: no remote copies, remote signals or barrier semaphores. Data moves between devices by JAX's collectives and lax.ppermute only.
A program may use at most 128 MiB of HBM per device.

v0:
```python
import jax
import jax.numpy as jnp
from jax import lax
from jax.sharding import PartitionSpec as P

BLOCK = 256
highest = lax.Precision.HIGHEST


def lower_inverse(lower_factor):
    order_size = lower_factor.shape[0]
    identity = jnp.eye(order_size, dtype=lower_factor.dtype)
    return lax.linalg.triangular_solve(lower_factor, identity, left_side=True, lower=True)


def contract_rows(left_rows, right_rows):
    return lax.dot_general(left_rows, right_rows, (((1,), (1,)), ((), ())), precision=highest)


def local(assembled, row_map, fill_pattern, trailing_block):
    wide_count = lax.axis_size("wide")
    col_count = lax.axis_size("col")
    asm_rows, twice_width = assembled.shape
    half_width = twice_width // 2
    trail_rows = trailing_block.shape[2]
    diag_share = twice_width // (col_count * wide_count)
    diag_col = twice_width // col_count
    wide_index = lax.axis_index("wide")
    col_index = lax.axis_index("col")
    device_index = wide_index * col_count + col_index
    packed_rows = (asm_rows + 1 + 7) // 8 * 8
    id_row = jnp.zeros((twice_width,), jnp.float32).at[:asm_rows].set(row_map.astype(jnp.float32))
    packed = jnp.concatenate(
        [
            assembled,
            id_row[None, :],
            jnp.zeros((packed_rows - asm_rows - 1, twice_width), jnp.float32),
        ],
        axis=0,
    )
    gathered = lax.all_gather(packed, "wide", axis=0, tiled=True)
    gathered3 = gathered.reshape(wide_count, packed_rows, twice_width)
    ids = gathered3[:, asm_rows, :asm_rows].astype(jnp.int32).reshape(-1)
    source = (
        jnp.arange(wide_count)[:, None] * packed_rows + jnp.arange(asm_rows)[None, :]
    ).reshape(-1)
    is_diagonal = ids < twice_width
    diag_slot = jnp.where(is_diagonal, ids - diag_col * col_index, diag_col)
    diag_src = jnp.zeros((diag_col,), jnp.int32).at[diag_slot].set(source, mode="drop")
    diag_block = gathered[diag_src]
    full = lax.all_gather(diag_block, "col", axis=0, tiled=True)
    trail_id = ids - twice_width
    owner_wide = trail_id // (trail_rows * col_count)
    trail_slot = jnp.where(
        is_diagonal, wide_count * trail_rows, owner_wide * trail_rows + trail_id % trail_rows
    )
    trail_src = (
        jnp.zeros((wide_count * trail_rows,), jnp.int32).at[trail_slot].set(source, mode="drop")
    )
    trail_all = gathered[trail_src]
    row_global = (
        (jnp.arange(wide_count)[:, None] * col_count + col_index) * trail_rows
        + jnp.arange(trail_rows)[None, :]
    ).reshape(-1)
    block_ids = row_global // BLOCK
    first_flags = fill_pattern[0][block_ids]
    second_flags = fill_pattern[1][block_ids]
    column_first = jnp.arange(twice_width) < half_width
    keep = jnp.where(column_first[None, :], first_flags[:, None], second_flags[:, None]).astype(
        jnp.float32
    )
    masked_all = trail_all * keep
    masked_own = lax.dynamic_slice_in_dim(masked_all, wide_index * trail_rows, trail_rows, 0)
    masked_range = lax.all_gather(masked_own, "col", axis=0, tiled=True)
    symmetric = (full + full.T) * 0.5
    factor = jnp.linalg.cholesky(symmetric)
    inverse = lower_inverse(factor)
    panel = contract_rows(masked_own, inverse)
    range_panel = contract_rows(masked_range, inverse)
    range_back = lax.dot_general(range_panel, inverse, (((1,), (0,)), ((), ())), precision=highest)
    update = contract_rows(masked_all, range_back)
    schur = trailing_block - update.reshape(trailing_block.shape)
    factor_rows = lax.dynamic_slice_in_dim(factor, device_index * diag_share, diag_share, 0)
    return (schur, panel, factor_rows)


def solution(mesh):
    in_specs = (P(("wide", "col"), None), P(("wide", "col")), P(), P(None, "col", None, "wide"))
    out_specs = (P(None, "col", None, "wide"), P(("wide", "col"), None), P(("wide", "col"), None))
    return jax.shard_map(local, mesh=mesh, in_specs=in_specs, out_specs=out_specs, check_vma=False)
```

profile of v0, /device:TPU:2, one launch (start us, length us, event | category | flops | bytes accessed | tf_op | source)
XLA Modules:
  0.0 598.0 jit_solution(17203450287779156365)
XLA Ops:
  9.9 90.4 %all-gather.4.cloned.1.call-done = f32[2560,1024]{1,0:T(8,128)} async-done(((f32[40,1024]{1,0:T(8,128)}), f32[2560,1024]{1,0:T(8,128)}) %all-gather.4.cloned.1.call-update) | async-done | bytes 10485776 | tf_op jit(solution)/shard_map/all_gather | solution.py:41
  101.8 9.0 %scatter_custom_fusion.1 = s32[256]{0:T(256)S(1)} fusion(s32[2304]{0:T(1024)S(1)} %get-tuple-element.23, s32[2304]{0:T(1024)S(1)} %reshape.468, s32[]{:T(128)} %copy.61), kind=kCustom, calls=%fused_computation.238 | custom fusion | bytes 1028 | tf_op jit(solution)/shard_map/scatter | solution.py:49
  133.1 15.6 %select_select_fusion.1 = s32[2048]{0:T(1024)S(1)} fusion(pred[2048]{0:T(1024)(128)(4,1)S(1)} %get-tuple-element.49, pred[2048]{0:T(1024)(128)(4,1)S(1)} %get-tuple-element.48, pred[2048]{0:T(1024)(128)(4,1)S(1)} %get-tuple-element.47, pred[2048]{0:T(1024)(128)(4,1)S(1)} %get-tuple-element.46, pred[2048]{0:T(1024)(128)(4,1)S(1)} %get-tuple-element.45, ...), kind=kLoop, calls=%fused_computation.212 | loop fusion | flops 51200 | bytes 67684 | tf_op jit(solution)/shard_map/gather | solution.py:67
  148.7 15.4 %select_select_fusion.2 = s32[2048]{0:T(1024)S(1)} fusion(pred[2048]{0:T(1024)(128)(4,1)S(1)} %get-tuple-element.49, pred[2048]{0:T(1024)(128)(4,1)S(1)} %get-tuple-element.48, pred[2048]{0:T(1024)(128)(4,1)S(1)} %get-tuple-element.47, pred[2048]{0:T(1024)(128)(4,1)S(1)} %get-tuple-element.46, pred[2048]{0:T(1024)(128)(4,1)S(1)} %get-tuple-element.45, ...), kind=kLoop, calls=%fused_computation.213 | loop fusion | flops 51200 | bytes 67684 | tf_op jit(solution)/shard_map/gather | solution.py:66
  164.2 9.0 %scatter_custom_fusion = s32[2048]{0:T(1024)S(1)} fusion(s32[2304]{0:T(1024)S(1)} %get-tuple-element.24, s32[2304]{0:T(1024)S(1)} %reshape.468, s32[]{:T(128)} %copy.61), kind=kCustom, calls=%fused_computation.216 | custom fusion | bytes 8196 | tf_op jit(solution)/shard_map/scatter | solution.py:58
  173.2 15.7 %gather_fusion = f32[2048,1024]{1,0:T(8,128)} fusion(f32[2560,1024]{1,0:T(8,128)} %all-gather.4.cloned.1.call-done, s32[2048]{0:T(1024)S(1)} %fusion.75), kind=kCustom, calls=%fused_computation | custom fusion | bytes 16785408 | tf_op jit(solution)/shard_map/gather | solution.py:60
  197.6 13.4 %all_gather.10 = f32[128,1024]{1,0:T(8,128)S(1)} all-gather(f32[32,1024]{1,0:T(8,128)S(1)} %constant_dynamic-slice_fusion.2), channel_id=1, replica_groups=mesh['wide'=64,'col'=4] {'col'}, dimensions={0}, use_global_device_ids=true | all-gather | bytes 655360 | tf_op jit(solution)/shard_map/all_gather | solution.py:74
  235.1 11.7 %cholesky.223 = f32[128,128]{1,0:T(8,128)S(1)} custom-call(f32[128,128]{1,0:T(8,128)S(1)} %cholesky.580), custom_call_target="Cholesky" | custom-call | tf_op jit(solution)/shard_map/jit(cholesky)/cholesky | solution.py:76
  249.3 9.8 %custom-call.62 = f32[1,128,128]{1,2,0:T(8,128)S(1)} custom-call(f32[1,128,128]{2,1,0:T(8,128)S(1)} %get-tuple-element.110), custom_call_target="InvertDiagBlocksLowerTriangular" | custom-call | tf_op jit(solution)/shard_map/jit(cholesky)/cholesky | solution.py:76
  263.0 12.1 %cholesky.244 = f32[128,128]{1,0:T(8,128)S(1)} custom-call(f32[128,128]{1,0:T(8,128)S(1)} %cholesky.584), custom_call_target="Cholesky" | custom-call | tf_op jit(solution)/shard_map/jit(cholesky)/cholesky | solution.py:76
  275.8 9.8 %custom-call.63 = f32[1,128,128]{1,2,0:T(8,128)S(1)} custom-call(f32[1,128,128]{2,1,0:T(8,128)S(1)} %get-tuple-element.107), custom_call_target="InvertDiagBlocksLowerTriangular" | custom-call | tf_op jit(solution)/shard_map/jit(cholesky)/cholesky | solution.py:76
  289.0 11.7 %cholesky.468 = f32[128,128]{1,0:T(8,128)S(1)} custom-call(f32[128,128]{1,0:T(8,128)S(1)} %cholesky.589), custom_call_target="Cholesky" | custom-call | tf_op jit(solution)/shard_map/jit(cholesky)/cholesky | solution.py:76
  302.0 9.8 %custom-call.64 = f32[1,128,128]{1,2,0:T(8,128)S(1)} custom-call(f32[1,128,128]{2,1,0:T(8,128)S(1)} %get-tuple-element.104), custom_call_target="InvertDiagBlocksLowerTriangular" | custom-call | tf_op jit(solution)/shard_map/jit(cholesky)/cholesky | solution.py:76
  315.4 11.8 %cholesky.487 = f32[128,128]{1,0:T(8,128)S(1)} custom-call(f32[128,128]{1,0:T(8,128)S(1)} %cholesky.594), custom_call_target="Cholesky" | custom-call | tf_op jit(solution)/shard_map/jit(cholesky)/cholesky | solution.py:76
  328.5 9.8 %custom-call.65 = f32[1,128,128]{1,2,0:T(8,128)S(1)} custom-call(f32[1,128,128]{2,1,0:T(8,128)S(1)} %get-tuple-element.101), custom_call_target="InvertDiagBlocksLowerTriangular" | custom-call | tf_op jit(solution)/shard_map/jit(cholesky)/cholesky | solution.py:76
  341.8 11.7 %cholesky.506 = f32[128,128]{1,0:T(8,128)S(1)} custom-call(f32[128,128]{1,0:T(8,128)S(1)} %cholesky.599), custom_call_target="Cholesky" | custom-call | tf_op jit(solution)/shard_map/jit(cholesky)/cholesky | solution.py:76
  354.8 10.0 %custom-call.66 = f32[1,128,128]{1,2,0:T(8,128)S(1)} custom-call(f32[1,128,128]{2,1,0:T(8,128)S(1)} %get-tuple-element.98), custom_call_target="InvertDiagBlocksLowerTriangular" | custom-call | tf_op jit(solution)/shard_map/jit(cholesky)/cholesky | solution.py:76
  368.1 11.7 %cholesky.526 = f32[128,128]{1,0:T(8,128)S(1)} custom-call(f32[128,128]{1,0:T(8,128)S(1)} %cholesky.604), custom_call_target="Cholesky" | custom-call | tf_op jit(solution)/shard_map/jit(cholesky)/cholesky | solution.py:76
  381.1 9.8 %custom-call.67 = f32[1,128,128]{1,2,0:T(8,128)S(1)} custom-call(f32[1,128,128]{2,1,0:T(8,128)S(1)} %get-tuple-element.95), custom_call_target="InvertDiagBlocksLowerTriangular" | custom-call | tf_op jit(solution)/shard_map/jit(cholesky)/cholesky | solution.py:76
  394.0 12.1 %cholesky.546 = f32[128,128]{1,0:T(8,128)S(1)} custom-call(f32[128,128]{1,0:T(8,128)S(1)} %cholesky.609), custom_call_target="Cholesky" | custom-call | tf_op jit(solution)/shard_map/jit(cholesky)/cholesky | solution.py:76
  407.4 9.8 %custom-call.68 = f32[1,128,128]{1,2,0:T(8,128)S(1)} custom-call(f32[1,128,128]{2,1,0:T(8,128)S(1)} %get-tuple-element.92), custom_call_target="InvertDiagBlocksLowerTriangular" | custom-call | tf_op jit(solution)/shard_map/jit(cholesky)/cholesky | solution.py:76
  419.8 11.7 %cholesky.564 = f32[128,128]{1,0:T(8,128)S(1)} custom-call(f32[128,128]{1,0:T(8,128)S(1)} %convolution_subtract_fusion.11), custom_call_target="Cholesky" | custom-call | tf_op jit(solution)/shard_map/jit(cholesky)/cholesky | solution.py:76
  445.1 23.2 %while.2 = (s32[]{:T(128)}, f32[1024,1024]{1,0:T(8,128)}, s32[8,2]{0,1:T(2,128)S(1)}, f32[8,128,128]{2,1,0:T(8,128)S(1)}, s32[]{:T(128)}) while((s32[]{:T(128)}, f32[1024,1024]{1,0:T(8,128)}, s32[8,2]{0,1:T(2,128)S(1)}, f32[8,128,128]{2,1,0:T(8,128)S(1)}, s32[]{:T(128)}) %tuple.153), condition=%wide.while_cond.1, body=%wide.while_body.1.sunk | while | flops 2 | bytes 131189 | solution.py:13
  468.3 78.8 %custom-call.69 = f32[8,128,128]{1,2,0:T(8,128)S(1)} custom-call(f32[8,128,128]{2,1,0:T(8,128)S(1)} %get-tuple-element.22), custom_call_target="InvertDiagBlocksLowerTriangular" | custom-call | tf_op jit(solution)/shard_map/triangular_solve | solution.py:13
  (144 shorter events, 167.0 us)
Async XLA Ops:
  7.2 93.1 %all-gather.4.cloned.1.call-start = ((), (), s32[]{:S(2)}) async-start(), calls=%async_computation | async-start | bytes 10649600 | tf_op jit(solution)/shard_map/all_gather | solution.py:41
  9.6 201.3 %all-gather.6.cloned.1.call-start = ((), (), s32[]{:S(2)}) async-start(), calls=%async_computation.1 | async-start | bytes 5242880 | tf_op jit(solution)/shard_map/all_gather | solution.py:51
  110.8 7.1 %copy-start.4 = (s32[2,32]{1,0:T(2,128)S(1)}, s32[2,32]{1,0:T(2,128)}, u32[]{:S(2)}) copy-start(s32[2,32]{1,0:T(2,128)} %param.8) | copy-start | bytes 772
  194.3 3.2 copy-start
  233.1 2.0 copy-start.2
  547.0 3.2 copy-start.1
  568.7 12.1 %slice-start = ((s8[8388608]{0:T(1024)(128)(4,1)}), s8[4194304]{0:T(1024)(128)(4,1)S(1)}, s32[]{:S(2)}) async-start(s8[8388608]{0:T(1024)(128)(4,1)} %bitcast.195), calls=%async_computation.2 | async-start | bytes 8388608
  574.0 6.9 %slice-start.1 = ((s8[8388608]{0:T(1024)(128)(4,1)}), s8[4194304]{0:T(1024)(128)(4,1)S(1)}, s32[]{:S(2)}) async-start(s8[8388608]{0:T(1024)(128)(4,1)} %bitcast.195), calls=%async_computation.3 | async-start | bytes 8388608
  580.9 8.7 %copy-start.3 = (f32[64,1,32,128]{3,2,1,0:T(8,128)S(1)}, f32[64,1,32,128]{3,2,1,0:T(8,128)}, u32[]{:S(2)}) copy-start(f32[64,1,32,128]{3,2,1,0:T(8,128)} %param.9) | copy-start | bytes 3145732
Sparse Core Ops, SparseCore 0:
  11.3 88.9 all-gather.3
  117.8 47.1 all-gather.5
where the time goes:
time: 607 us; the launch traced here: 598 us
  other arithmetic  322 us (53%)
  waiting for transfers between devices  90.4 us (15%)
  local copies, waits for them, and re-layouts  88 us (14%)
  matrix products  64 us (11%)
  between operations  20.1 us (3%)
  blocking collectives  13.4 us (2%)
    another operation x30, other arithmetic, local(): factor = jnp.linalg.cholesky(symmetric)  173 us
    all_gather x1, waiting for transfers between devices, local(): gathered = lax.all_gather(packed, 'wide', axis=0, tiled=True)  90.4 us
    another operation x3, other arithmetic, lower_inverse(): lax.linalg.triangular_solve(lower_factor, identity, left_side=True, lower...  85.4 us
    another operation x14, matrix products, local(): factor = jnp.linalg.cholesky(symmetric)  23.1 us
    another operation x24, local copies, waits for them, and re-layouts  23 us
    another operation x15, matrix products, lower_inverse(): lax.linalg.triangular_solve(lower_factor, identity, left_side=True, lower...  22.2 us
    gather x3, other arithmetic, local(): first_flags = fill_pattern[0][block_ids]  20.6 us
    gather x2, other arithmetic, local(): second_flags = fill_pattern[1][block_ids]  19.9 us
  transfers between devices with their start and end apart: 2, of which 1 were waited for; matrix products, arithmetic and copies ran while one was open for 13% of the time, Pallas kernels for 0%

commit v1 on v0

--- a/solution.py
+++ b/solution.py
@@ -38,7 +38,9 @@
         ],
         axis=0,
     )
-    gathered = lax.all_gather(packed, "wide", axis=0, tiled=True)
+    gathered = jnp.concatenate(
+        lax.all_to_all(jnp.stack([packed] * lax.axis_size("wide")), "wide", 0, 0), axis=0
+    )
     gathered3 = gathered.reshape(wide_count, packed_rows, twice_width)
     ids = gathered3[:, asm_rows, :asm_rows].astype(jnp.int32).reshape(-1)
     source = (

time: 607 us -> 766 us (1.26)
  waiting for transfers between devices: 90.4 us -> 229 us
  starting transfers between devices: 0.08 us -> 12.4 us
    all_to_all x0 -> x1, waiting for transfers between devices: none -> 229 us  [local(): lax.all_to_all(jnp.stack([packed] * lax.axis_size('wide')), 'wide', 0, 0)]
    all_gather x1 -> x0, waiting for transfers between devices: 90.4 us -> none  [local(): gathered = lax.all_gather(packed, 'wide', axis=0, tiled=True)]
    all_to_all x0 -> x1, starting transfers between devices: none -> 12.3 us  [local(): lax.all_to_all(jnp.stack([packed] * lax.axis_size('wide')), 'wide', 0, 0)]
    another operation x24 -> x25, local copies, waits for them, and re-layouts: 23 us -> 28.2 us
  transfers between devices with their start and end apart: 2 -> 2, of which waited for: 1 -> 1; matrix products, arithmetic and copies ran while one was open for 13% -> 10% of each run, Pallas kernels for 0% -> 0%
where the time goes in v1:
time: 766 us; the launch traced here: 755 us
  other arithmetic  323 us (42%)
  waiting for transfers between devices  229 us (30%)
  local copies, waits for them, and re-layouts  92.2 us (12%)
  matrix products  64 us (8%)
  between operations  20.1 us (3%)
  blocking collectives  13.4 us (2%)
  starting transfers between devices  12.4 us (2%)
    all_to_all x1, waiting for transfers between devices, local(): lax.all_to_all(jnp.stack([packed] * lax.axis_size('wide')), 'wide', 0, 0)  229 us
    another operation x30, other arithmetic, local(): factor = jnp.linalg.cholesky(symmetric)  173 us
    another operation x3, other arithmetic, lower_inverse(): lax.linalg.triangular_solve(lower_factor, identity, left_side=True, lower...  85.4 us
    another operation x14, matrix products, local(): factor = jnp.linalg.cholesky(symmetric)  23.1 us
    another operation x24, local copies, waits for them, and re-layouts  23 us
    another operation x15, matrix products, lower_inverse(): lax.linalg.triangular_solve(lower_factor, identity, left_side=True, lower...  22.2 us
    gather x3, other arithmetic, local(): first_flags = fill_pattern[0][block_ids]  20.6 us
    gather x2, other arithmetic, local(): second_flags = fill_pattern[1][block_ids]  19.9 us
  transfers between devices with their start and end apart: 2, of which 1 were waited for; matrix products, arithmetic and copies ran while one was open for 10% of the time, Pallas kernels for 0%

profile of v1, /device:TPU:2, one launch (start us, length us, event | category | flops | bytes accessed | tf_op | source)
XLA Modules:
  0.0 754.9 jit_solution(9869255326954131240)
XLA Ops:
  14.1 12.3 %all-to-all-start = ((f32[64,40,1024]{2,1,0:T(8,128)}), f32[64,40,1024]{2,1,0:T(8,128)}, u32[]{:S(2)}, u32[]{:S(2)}) async-start(f32[64,40,1024]{2,1,0:T(8,128)} %stack.2), calls=%async_computation | async-start | bytes 20971520 | tf_op jit(solution)/shard_map/all_to_all | solution.py:42
  26.7 229.3 %all-to-all-done = f32[64,40,1024]{2,1,0:T(8,128)} async-done(((f32[64,40,1024]{2,1,0:T(8,128)}), f32[64,40,1024]{2,1,0:T(8,128)}, u32[]{:S(2)}, u32[]{:S(2)}) %all-to-all-start) | async-done | bytes 10485792 | tf_op jit(solution)/shard_map/all_to_all | solution.py:42
  290.0 15.6 %select_select_fusion.1 = s32[2048]{0:T(1024)S(1)} fusion(pred[2048]{0:T(1024)(128)(4,1)S(1)} %get-tuple-element.51, pred[2048]{0:T(1024)(128)(4,1)S(1)} %get-tuple-element.50, pred[2048]{0:T(1024)(128)(4,1)S(1)} %get-tuple-element.49, pred[2048]{0:T(1024)(128)(4,1)S(1)} %get-tuple-element.48, pred[2048]{0:T(1024)(128)(4,1)S(1)} %get-tuple-element.47, ...), kind=kLoop, calls=%fused_computation.213 | loop fusion | flops 51200 | bytes 67684 | tf_op jit(solution)/shard_map/gather | solution.py:69
  305.7 15.5 %select_select_fusion.2 = s32[2048]{0:T(1024)S(1)} fusion(pred[2048]{0:T(1024)(128)(4,1)S(1)} %get-tuple-element.51, pred[2048]{0:T(1024)(128)(4,1)S(1)} %get-tuple-element.50, pred[2048]{0:T(1024)(128)(4,1)S(1)} %get-tuple-element.49, pred[2048]{0:T(1024)(128)(4,1)S(1)} %get-tuple-element.48, pred[2048]{0:T(1024)(128)(4,1)S(1)} %get-tuple-element.47, ...), kind=kLoop, calls=%fused_computation.214 | loop fusion | flops 51200 | bytes 67684 | tf_op jit(solution)/shard_map/gather | solution.py:68
  321.1 9.0 %scatter_custom_fusion = s32[2048]{0:T(1024)S(1)} fusion(s32[2304]{0:T(1024)S(1)} %get-tuple-element.26, s32[2304]{0:T(1024)S(1)} %reshape.470, s32[]{:T(128)} %copy.64), kind=kCustom, calls=%fused_computation.217 | custom fusion | bytes 8196 | tf_op jit(solution)/shard_map/scatter | solution.py:60
  330.1 15.7 %gather_fusion = f32[2048,1024]{1,0:T(8,128)} fusion(f32[2560,1024]{1,0:T(8,128)} %bitcast.1, s32[2048]{0:T(1024)S(1)} %fusion.75), kind=kCustom, calls=%fused_computation | custom fusion | bytes 16785408 | tf_op jit(solution)/shard_map/gather | solution.py:62
  354.5 13.4 %all_gather.6 = f32[128,1024]{1,0:T(8,128)S(1)} all-gather(f32[32,1024]{1,0:T(8,128)S(1)} %constant_dynamic-slice_fusion.2), channel_id=1, replica_groups=mesh['wide'=64,'col'=4] {'col'}, dimensions={0}, use_global_device_ids=true | all-gather | bytes 655360 | tf_op jit(solution)/shard_map/all_gather | solution.py:76
  392.0 11.7 %cholesky.223 = f32[128,128]{1,0:T(8,128)S(1)} custom-call(f32[128,128]{1,0:T(8,128)S(1)} %cholesky.580), custom_call_target="Cholesky" | custom-call | tf_op jit(solution)/shard_map/jit(cholesky)/cholesky | solution.py:78
  406.2 9.8 %custom-call.62 = f32[1,128,128]{1,2,0:T(8,128)S(1)} custom-call(f32[1,128,128]{2,1,0:T(8,128)S(1)} %get-tuple-element.112), custom_call_target="InvertDiagBlocksLowerTriangular" | custom-call | tf_op jit(solution)/shard_map/jit(cholesky)/cholesky | solution.py:78
  420.0 12.1 %cholesky.244 = f32[128,128]{1,0:T(8,128)S(1)} custom-call(f32[128,128]{1,0:T(8,128)S(1)} %cholesky.584), custom_call_target="Cholesky" | custom-call | tf_op jit(solution)/shard_map/jit(cholesky)/cholesky | solution.py:78
  432.7 9.8 %custom-call.63 = f32[1,128,128]{1,2,0:T(8,128)S(1)} custom-call(f32[1,128,128]{2,1,0:T(8,128)S(1)} %get-tuple-element.109), custom_call_target="InvertDiagBlocksLowerTriangular" | custom-call | tf_op jit(solution)/shard_map/jit(cholesky)/cholesky | solution.py:78
  445.9 11.7 %cholesky.468 = f32[128,128]{1,0:T(8,128)S(1)} custom-call(f32[128,128]{1,0:T(8,128)S(1)} %cholesky.589), custom_call_target="Cholesky" | custom-call | tf_op jit(solution)/shard_map/jit(cholesky)/cholesky | solution.py:78
  458.9 9.8 %custom-call.64 = f32[1,128,128]{1,2,0:T(8,128)S(1)} custom-call(f32[1,128,128]{2,1,0:T(8,128)S(1)} %get-tuple-element.106), custom_call_target="InvertDiagBlocksLowerTriangular" | custom-call | tf_op jit(solution)/shard_map/jit(cholesky)/cholesky | solution.py:78
  472.3 11.8 %cholesky.487 = f32[128,128]{1,0:T(8,128)S(1)} custom-call(f32[128,128]{1,0:T(8,128)S(1)} %cholesky.594), custom_call_target="Cholesky" | custom-call | tf_op jit(solution)/shard_map/jit(cholesky)/cholesky | solution.py:78
  485.4 9.8 %custom-call.65 = f32[1,128,128]{1,2,0:T(8,128)S(1)} custom-call(f32[1,128,128]{2,1,0:T(8,128)S(1)} %get-tuple-element.103), custom_call_target="InvertDiagBlocksLowerTriangular" | custom-call | tf_op jit(solution)/shard_map/jit(cholesky)/cholesky | solution.py:78
  498.7 11.7 %cholesky.506 = f32[128,128]{1,0:T(8,128)S(1)} custom-call(f32[128,128]{1,0:T(8,128)S(1)} %cholesky.599), custom_call_target="Cholesky" | custom-call | tf_op jit(solution)/shard_map/jit(cholesky)/cholesky | solution.py:78
  511.7 10.0 %custom-call.66 = f32[1,128,128]{1,2,0:T(8,128)S(1)} custom-call(f32[1,128,128]{2,1,0:T(8,128)S(1)} %get-tuple-element.100), custom_call_target="InvertDiagBlocksLowerTriangular" | custom-call | tf_op jit(solution)/shard_map/jit(cholesky)/cholesky | solution.py:78
  525.0 11.7 %cholesky.526 = f32[128,128]{1,0:T(8,128)S(1)} custom-call(f32[128,128]{1,0:T(8,128)S(1)} %cholesky.604), custom_call_target="Cholesky" | custom-call | tf_op jit(solution)/shard_map/jit(cholesky)/cholesky | solution.py:78
  538.0 9.8 %custom-call.67 = f32[1,128,128]{1,2,0:T(8,128)S(1)} custom-call(f32[1,128,128]{2,1,0:T(8,128)S(1)} %get-tuple-element.97), custom_call_target="InvertDiagBlocksLowerTriangular" | custom-call | tf_op jit(solution)/shard_map/jit(cholesky)/cholesky | solution.py:78
  550.9 12.1 %cholesky.546 = f32[128,128]{1,0:T(8,128)S(1)} custom-call(f32[128,128]{1,0:T(8,128)S(1)} %cholesky.609), custom_call_target="Cholesky" | custom-call | tf_op jit(solution)/shard_map/jit(cholesky)/cholesky | solution.py:78
  564.3 9.8 %custom-call.68 = f32[1,128,128]{1,2,0:T(8,128)S(1)} custom-call(f32[1,128,128]{2,1,0:T(8,128)S(1)} %get-tuple-element.94), custom_call_target="InvertDiagBlocksLowerTriangular" | custom-call | tf_op jit(solution)/shard_map/jit(cholesky)/cholesky | solution.py:78
  576.7 11.7 %cholesky.564 = f32[128,128]{1,0:T(8,128)S(1)} custom-call(f32[128,128]{1,0:T(8,128)S(1)} %convolution_subtract_fusion.11), custom_call_target="Cholesky" | custom-call | tf_op jit(solution)/shard_map/jit(cholesky)/cholesky | solution.py:78
  602.0 23.2 %while.2 = (s32[]{:T(128)}, f32[1024,1024]{1,0:T(8,128)}, s32[8,2]{0,1:T(2,128)S(1)}, f32[8,128,128]{2,1,0:T(8,128)S(1)}, s32[]{:T(128)}) while((s32[]{:T(128)}, f32[1024,1024]{1,0:T(8,128)}, s32[8,2]{0,1:T(2,128)S(1)}, f32[8,128,128]{2,1,0:T(8,128)S(1)}, s32[]{:T(128)}) %tuple.153), condition=%wide.while_cond.1, body=%wide.while_body.1.sunk | while | flops 2 | bytes 131189 | solution.py:13
  625.2 78.8 %custom-call.69 = f32[8,128,128]{1,2,0:T(8,128)S(1)} custom-call(f32[8,128,128]{2,1,0:T(8,128)S(1)} %get-tuple-element.22), custom_call_target="InvertDiagBlocksLowerTriangular" | custom-call | tf_op jit(solution)/shard_map/triangular_solve | solution.py:13
  (143 shorter events, 181.7 us)
Async XLA Ops:
  14.1 241.9 %all-to-all-start = ((f32[64,40,1024]{2,1,0:T(8,128)}), f32[64,40,1024]{2,1,0:T(8,128)}, u32[]{:S(2)}, u32[]{:S(2)}) async-start(f32[64,40,1024]{2,1,0:T(8,128)} %stack.2), calls=%async_computation | async-start | bytes 20971520 | tf_op jit(solution)/shard_map/all_to_all | solution.py:42
  26.4 341.4 %all-gather.3.cloned.1.call-start = ((), (), s32[]{:S(2)}) async-start(), calls=%async_computation.1 | async-start | bytes 5242880 | tf_op jit(solution)/shard_map/all_gather | solution.py:53
  267.7 7.1 copy-start.4
  351.3 3.2 copy-start
  390.0 2.0 copy-start.2
  703.9 3.2 copy-start.1
  725.6 12.1 %slice-start = ((s8[8388608]{0:T(1024)(128)(4,1)}), s8[4194304]{0:T(1024)(128)(4,1)S(1)}, s32[]{:S(2)}) async-start(s8[8388608]{0:T(1024)(128)(4,1)} %bitcast.187), calls=%async_computation.2 | async-start | bytes 8388608
  730.9 6.9 slice-start.1
  737.8 8.7 %copy-start.3 = (f32[64,1,32,128]{3,2,1,0:T(8,128)S(1)}, f32[64,1,32,128]{3,2,1,0:T(8,128)}, u32[]{:S(2)}) copy-start(f32[64,1,32,128]{3,2,1,0:T(8,128)} %param.9) | copy-start | bytes 3145732
Sparse Core Ops, SparseCore 0:
  274.7 47.8 all-gather.2
